TPU v7x, 768 devices: a whole 4x8x12 slice. The times are simulated.
768 devices in a mesh: ctx: 16 (over x_hi, y), tp: 48 (over x_lo, z, core).
Axes of the slice: x: 4 (x_hi: 2, x_lo: 2; x = x_hi * 2 + x_lo), y: 8, z: 12, core: 2. Of those that a mesh axis runs over, the one named last changes fastest.
Arguments:
- projected: bfloat16 [3, 4096, 6144], P(None, 'ctx', 'tp'), may hold values from -6 to 6
- filters: float32 [384, 128], P('tp'), may hold values from -0.5 to 0.5
- out_weight: bfloat16 [6144, 6144], P('tp'), may hold values from -0.1875 to 0.1875
- grad_out: bfloat16 [4096, 6144], P('ctx', 'tp'), may hold values from -6 to 6
Outputs:
- block_out: bfloat16 [4096, 6144], P('ctx', 'tp')
- grad_inputs: bfloat16 [3, 4096, 6144], P(None, 'ctx', 'tp')
- grad_weight: float32 [6144, 6144], P('tp', 'ctx')
- grad_filters: float32 [384, 128], P('tp', 'ctx')
All inputs are finite; a program needn't handle non-finite values.
Results may differ from a plain program's by a relative error of at most 0.0064.
Values may be sent and summed in bfloat16 or wider, within the bound.
No kernel may reach another device: no remote copies, remote signals or barrier semaphores. Data moves between devices by JAX's collectives and lax.ppermute only.
A program may use at most 64 MiB of HBM per device.

v0:
```python
import math

import jax
import jax.numpy as jnp
from jax import lax
from jax.sharding import Mesh, PartitionSpec as P


GATHER_BY_A2A = False


def shifted(value, axis, steps):
    count = lax.axis_size(axis)
    first, last = (max(0, -steps), min(count, count - steps))
    return lax.ppermute(value, axis, [(source, source + steps) for source in range(first, last)])


def toeplitz_blocks(tap_values, out_rows, ahead=False):
    groups, taps_count = tap_values.shape
    extent = taps_count + out_rows
    left_zeros = jnp.zeros((groups, out_rows), tap_values.dtype)
    right_zeros = jnp.zeros((groups, out_rows), tap_values.dtype)
    ordered = tap_values if ahead else tap_values[:, ::-1]
    padded = jnp.concatenate([left_zeros, ordered, right_zeros], axis=1)
    length_all = padded.shape[1]
    rolled = jnp.roll(padded, -out_rows if ahead else -(out_rows - 1), axis=1)
    tiled = jnp.tile(rolled, (1, out_rows))
    sheared = tiled[:, : out_rows * (length_all - 1)].reshape(groups, out_rows, length_all - 1)
    return sheared[:, :, :extent]


def summed_exchange(parts, axis):
    sent = parts.astype(jnp.bfloat16)
    got = lax.all_to_all(sent, axis, 0, 0)
    return jnp.sum(got.astype(jnp.float32), axis=0)


def local(projected, filters, out_weight, grad_out):
    out_rows = projected.shape[1]
    channels = projected.shape[2]
    groups, taps_count = filters.shape
    group_size = channels // groups
    extent = taps_count + out_rows
    chips = lax.axis_size("tpo")
    cores = lax.axis_size("core")
    tp_count = chips * cores
    ctx_count = lax.axis_size("ctx")
    features = out_weight.shape[1]
    query_rows = projected[0].astype(jnp.float32)
    key_rows = projected[1].astype(jnp.float32)
    value_rows = projected[2].astype(jnp.float32)
    gated_rows = (key_rows * value_rows).astype(jnp.bfloat16)
    earlier = shifted(gated_rows[out_rows - taps_count :], "ctx", 1)
    extended = jnp.concatenate([earlier, gated_rows], axis=0).reshape(extent, groups, group_size)
    taps = filters.astype(jnp.bfloat16)
    blocks = toeplitz_blocks(taps, out_rows)
    filtered = jnp.einsum(
        "gts,sgc->tgc", blocks, extended, preferred_element_type=jnp.float32
    ).reshape(out_rows, channels)
    mixed_rows = (query_rows * filtered).astype(jnp.bfloat16)
    partial_out = jnp.einsum("cd,tc->dt", out_weight, mixed_rows, preferred_element_type=jnp.float32)
    block = features // tp_count
    halves = partial_out.reshape(chips, cores, block, out_rows)
    pair = lax.all_to_all(halves, "core", 1, 1)
    chip_sum = jnp.sum(pair, axis=1)
    own_features = summed_exchange(chip_sum, "tpo")
    block_out = own_features.T.astype(jnp.bfloat16)
    if GATHER_BY_A2A:
        copies = jnp.broadcast_to(grad_out[None], (tp_count,) + grad_out.shape)
        pieces = lax.all_to_all(copies, "tp", 0, 0)
        full_grad = jnp.transpose(pieces, (1, 0, 2)).reshape(out_rows, features)
    else:
        same_core = lax.all_gather(grad_out, "tpo", axis=0)
        partner = lax.ppermute(same_core, "core", [(0, 1), (1, 0)])
        first = lax.axis_index("core") == 0
        both = jnp.stack([jnp.where(first, same_core, partner), jnp.where(first, partner, same_core)], axis=2)
        full_grad = jnp.transpose(both, (1, 0, 2, 3)).reshape(out_rows, features)
    block_out, full_grad = lax.optimization_barrier((block_out, full_grad))
    grad_mixed = jnp.einsum("td,cd->tc", full_grad, out_weight, preferred_element_type=jnp.float32)
    grad_filtered = (grad_mixed * query_rows).astype(jnp.bfloat16)
    grad_query = (grad_mixed * filtered).astype(jnp.bfloat16)
    following = shifted(grad_filtered[:taps_count], "ctx", -1)
    ahead_rows = jnp.concatenate([grad_filtered, following], axis=0).reshape(
        extent, groups, group_size
    )
    grad_gated = jnp.einsum(
        "gts,sgc->tgc", toeplitz_blocks(taps, out_rows, ahead=True), ahead_rows, preferred_element_type=jnp.float32
    ).reshape(out_rows, channels)
    flipped = jnp.einsum(
        "tgc,sgc->gts",
        grad_filtered.reshape(out_rows, groups, group_size),
        jnp.pad(extended[::-1], ((0, 1), (0, 0), (0, 0))),
        preferred_element_type=jnp.float32,
    )
    flattened = flipped.reshape(groups, out_rows * (extent + 1))
    diagonals = flattened[:, out_rows - 1 : out_rows - 1 + out_rows * extent].reshape(
        groups, out_rows, extent
    )[:, :, :taps_count]
    sequence = ctx_count * out_rows
    filter_term = jnp.sum(diagonals, axis=1) / math.sqrt(sequence * group_size)
    weight_scale = 1.0 / math.sqrt(sequence)
    weight_term = (
        jnp.einsum("tc,td->dc", mixed_rows, full_grad, preferred_element_type=jnp.float32)
        * weight_scale
    )
    own_cols = features // ctx_count
    own_taps = taps_count // ctx_count
    weight_parts = weight_term.reshape(ctx_count, own_cols, channels)
    filter_parts = jnp.transpose(filter_term.reshape(groups, ctx_count, own_taps), (1, 0, 2))
    filter_rows = jnp.pad(filter_parts, ((0, 0), (0, 0), (0, channels - own_taps)))
    packed = jnp.concatenate([weight_parts, filter_rows], axis=1)
    packed, _ = lax.optimization_barrier((packed, following))
    summed = summed_exchange(packed, "ctx")
    grad_weight = summed[:own_cols].T
    grad_filters = summed[own_cols:, :own_taps]
    grad_key = (grad_gated * value_rows).astype(jnp.bfloat16)
    grad_value = (grad_gated * key_rows).astype(jnp.bfloat16)
    grad_inputs = jnp.stack([grad_query, grad_key, grad_value])
    return (block_out, grad_inputs, grad_weight, grad_filters)


def solution(mesh):
    tp_count = mesh.shape["tp"]
    split = Mesh(mesh.devices.reshape(mesh.shape["ctx"], tp_count // 2, 2), ("ctx", "tpo", "core"))
    tp = ("tpo", "core")
    placed = (P(None, "ctx", tp), P(tp, None), P(tp, None), P("ctx", tp))
    return jax.shard_map(
        local,
        mesh=split,
        in_specs=placed,
        out_specs=(P("ctx", tp), P(None, "ctx", tp), P(tp, "ctx"), P(tp, "ctx")),
        check_vma=False,
    )
```

profile of v0, /device:TPU:10, one launch (start us, length us, event | category | flops | bytes accessed | tf_op | source)
XLA Modules:
  0.0 227.5 jit_solution(16663335017204120138)
XLA Ops:
  8.5 3.5 %collective-permute-start = (bf16[128,128]{0,1:T(8,128)(2,1)S(1)}, bf16[128,128]{0,1:T(8,128)(2,1)S(1)}, u32[]{:S(2)}, u32[]{:S(2)}) collective-permute-start(bf16[128,128]{0,1:T(8,128)(2,1)S(1)} %slice_bitcast_fusion.1), channel_id=1, source_target_pairs={{0,48},{48,96},{96,144},{144,192},{192,240},{240,288},{288,336},{3... | collective-permute-start | bytes 98312 | tf_op jit(solution)/shard_map/ppermute | solution.py:15
  13.1 1.6 slice.73
  14.8 7.2 %reshape.79 = bf16[1308672]{0:T(1024)(128)(2,1)} reshape(bf16[8,163584]{1,0:T(8,128)(2,1)} %slice.73) | data formatting | bytes 5234688
  21.9 8.2 %reshape.66 = bf16[8,256,639]{2,1,0:T(8,128)(2,1)} reshape(bf16[1308672]{0:T(1024)(128)(2,1)} %reshape.79) | data formatting | bytes 5234688 | tf_op jit(solution)/shard_map/reshape | solution.py:28
  30.3 1.9 fusion.2
  32.3 3.7 %convolution_bitcast_fusion = f32[6144,256]{0,1:T(8,128)} fusion(bf16[256,128]{0,1:T(8,128)(2,1)S(1)} %fusion.7, bf16[128,6144]{1,0:T(8,128)(2,1)S(1)} %copy-done), kind=kOutput, calls=%fused_computation | convolution fusion | flops 402653184 | bytes 7929856 | tf_op jit(solution)/shard_map/cd,tc->dt/dot_general | solution.py:61
  35.9 9.0 %reshape.68 = f32[24,2,128,256]{2,1,0,3:T(2,128)} reshape(f32[6144,256]{0,1:T(8,128)} %convolution_bitcast_fusion) | data formatting | bytes 12582912 | tf_op jit(solution)/shard_map/reshape | solution.py:63
  44.9 3.2 %copy.42 = f32[24,2,128,256]{2,0,3,1:T(8,128)S(1)} copy(f32[24,2,128,256]{2,1,0,3:T(2,128)} %reshape.68) | data formatting | bytes 12582912 | tf_op jit(solution)/shard_map/reshape | solution.py:63
  48.1 10.0 %all_to_all.15 = f32[24,2,128,256]{2,0,3,1:T(8,128)} all-to-all(f32[24,2,128,256]{2,0,3,1:T(8,128)S(1)} %copy.42), channel_id=1, replica_groups=mesh['ctx'=16,'tpo'=24,'core'=2] {'core'}, dimensions={1} | all-to-all | bytes 12582912 | tf_op jit(solution)/shard_map/all_to_all | solution.py:64
  58.0 3.5 %reduce_sum.39 = bf16[24,128,256]{1,0,2:T(8,128)(2,1)S(1)} reduce(f32[24,2,128,256]{2,0,3,1:T(8,128)} %all_to_all.15, f32[]{:T(128)} %constant.5.clone.1), dimensions={1}, to_apply=%region_0.1 | reduce | flops 786432 | bytes 7864324 | tf_op jit(solution)/shard_map/reduce_sum | solution.py:65
  61.5 1.5 copy.44
  63.0 16.7 %all-to-all-start.1 = ((bf16[24,128,256]{1,2,0:T(8,128)(2,1)}), bf16[24,128,256]{1,2,0:T(8,128)(2,1)S(1)}, u32[]{:S(2)}, u32[]{:S(2)}) async-start(bf16[24,128,256]{1,2,0:T(8,128)(2,1)} %copy.44), calls=%async_computation.1 | async-start | bytes 3145728 | tf_op jit(solution)/shard_map/all_to_all | solution.py:34
  79.7 54.2 %all-gather.3.cloned.1.call-done = bf16[6144,128]{1,0:T(8,128)(2,1)} async-done(((bf16[256,128]{1,0:T(8,128)(2,1)}), bf16[6144,128]{1,0:T(8,128)(2,1)}) %all-gather.3.cloned.1.call-update) | async-done | bytes 1572880 | tf_op jit(solution)/shard_map/all_gather | solution.py:73
  133.9 1.9 collective-permute-start.1
  135.9 1.4 rev.7
  137.3 3.0 %all-to-all-done.1 = bf16[24,128,256]{1,2,0:T(8,128)(2,1)S(1)} async-done(((bf16[24,128,256]{1,2,0:T(8,128)(2,1)}), bf16[24,128,256]{1,2,0:T(8,128)(2,1)S(1)}, u32[]{:S(2)}, u32[]{:S(2)}) %all-to-all-start.1) | async-done | bytes 1572896 | tf_op jit(solution)/shard_map/all_to_all | solution.py:34
  141.2 2.1 select_bitcast_fusion.1
  143.3 2.0 maximum_bitcast_fusion
  145.2 4.6 %copy.45 = bf16[256,24,2,128]{0,3,2,1:T(8,128)(2,1)} copy(bf16[256,24,2,128]{3,0,1,2:T(8,128)(2,1)} %maximum_bitcast_fusion) | data formatting | bytes 6291456 | tf_op jit(solution)/shard_map/transpose | solution.py:77
  149.9 3.2 %fusion.9 = (bf16[256,128]{0,1:T(8,128)(2,1)}, bf16[256,128]{0,1:T(8,128)(2,1)S(1)}) fusion(f32[8,16,256]{2,1,0:T(8,128)S(1)} %fusion.2, bf16[1,256,128]{1,2,0:T(8,128)(2,1)S(1)} %copy.52, bf16[128,6144]{1,0:T(8,128)(2,1)S(1)} %copy-done, bf16[256,6144]{0,1:T(8,128)(2,1)} %bitcast.52), kind=kOutput, calls=%fused_computation.26 | convolution fusion | flops 402817024 | bytes 5046272 | tf_op jit(solution)/shard_map/td,cd->tc/dot_general | solution.py:79
  154.1 2.6 %fusion.10 = f32[8,256,385]{2,1,0:T(8,128)} fusion(bf16[256,8,16]{0,2,1:T(8,128)(2,1)S(1)} %bitcast.62, bf16[384,8,16]{0,2,1:T(8,128)(2,1)S(1)} %copy-done.6), kind=kOutput, calls=%fused_computation.27 | convolution fusion | flops 25231360 | bytes 3317760 | tf_op jit(solution)/shard_map/tgc,sgc->gts/dot_general | solution.py:89
  156.8 5.8 %reshape.75 = f32[8,98560]{1,0:T(8,128)} reshape(f32[8,256,385]{2,1,0:T(8,128)} %fusion.10) | data formatting | bytes 6307840 | tf_op jit(solution)/shard_map/reshape | solution.py:95
  162.5 2.8 %slice.78 = f32[8,98304]{1,0:T(8,128)S(1)} slice(f32[8,98560]{1,0:T(8,128)} %reshape.75), slice={[0:8], [255:98559]} | slice | bytes 6291456 | tf_op jit(solution)/shard_map/slice | solution.py:96
  165.7 2.2 collective-permute-start.2
  168.0 1.3 select_maximum_fusion
  169.3 2.2 collective-permute-done.2
  171.5 8.7 %all-to-all-start.2 = ((bf16[16,392,128]{2,1,0:T(8,128)(2,1)}), bf16[16,392,128]{2,1,0:T(8,128)(2,1)S(1)}, u32[]{:S(2)}, u32[]{:S(2)}) async-start(bf16[16,392,128]{2,1,0:T(8,128)(2,1)} %select_maximum_fusion), calls=%async_computation.2 | async-start | bytes 3211264 | tf_op jit(solution)/shard_map/all_to_all | solution.py:34
  180.4 1.6 slice.76
  182.1 7.1 %reshape.81 = bf16[1308672]{0:T(1024)(128)(2,1)} reshape(bf16[8,163584]{1,0:T(8,128)(2,1)} %slice.76) | data formatting | bytes 5234688
  189.2 8.3 %reshape.71 = bf16[8,256,639]{2,1,0:T(8,128)(2,1)} reshape(bf16[1308672]{0:T(1024)(128)(2,1)} %reshape.81) | data formatting | bytes 5234688 | tf_op jit(solution)/shard_map/reshape | solution.py:28
  197.5 1.9 fusion
  200.3 18.6 %all-to-all-done.2 = bf16[16,392,128]{2,1,0:T(8,128)(2,1)S(1)} async-done(((bf16[16,392,128]{2,1,0:T(8,128)(2,1)}), bf16[16,392,128]{2,1,0:T(8,128)(2,1)S(1)}, u32[]{:S(2)}, u32[]{:S(2)}) %all-to-all-start.2) | async-done | bytes 1605664 | tf_op jit(solution)/shard_map/all_to_all | solution.py:34
  (50 shorter events, 7.5 us)
Async XLA Ops:
  7.2 25.1 %copy-start = (bf16[128,6144]{1,0:T(8,128)(2,1)S(1)}, bf16[128,6144]{1,0:T(8,128)(2,1)}, u32[]{:S(2)}) copy-start(bf16[128,6144]{1,0:T(8,128)(2,1)} %param.6) | copy-start | bytes 4718596
  7.2 126.8 %all-gather.3.cloned.1.call-start = ((), (), s32[]{:S(2)}) async-start(), calls=%async_computation.3 | async-start | bytes 1638400 | tf_op jit(solution)/shard_map/all_gather | solution.py:73
  8.4 6.4 %copy-start.2 = (bf16[1,256,128]{1,2,0:T(8,128)(2,1)}, bf16[1,256,128]{1,2,0:T(8,128)(2,1)S(1)}, u32[]{:S(2)}) copy-start(bf16[1,256,128]{1,2,0:T(8,128)(2,1)S(1)} %copy.53) | copy-start | bytes 196612
  8.5 6.3 %copy-start.4 = (bf16[1,256,128]{1,2,0:T(8,128)(2,1)}, bf16[1,256,128]{1,2,0:T(8,128)(2,1)S(1)}, u32[]{:S(2)}) copy-start(bf16[1,256,128]{1,2,0:T(8,128)(2,1)S(1)} %copy.54) | copy-start | bytes 196612
  8.5 21.7 %collective-permute-start = (bf16[128,128]{0,1:T(8,128)(2,1)S(1)}, bf16[128,128]{0,1:T(8,128)(2,1)S(1)}, u32[]{:S(2)}, u32[]{:S(2)}) collective-permute-start(bf16[128,128]{0,1:T(8,128)(2,1)S(1)} %slice_bitcast_fusion.1), channel_id=1, source_target_pairs={{0,48},{48,96},{96,144},{144,192},{192,240},{240,288},{288,336},{3... | collective-permute-start | bytes 98312 | tf_op jit(solution)/shard_map/ppermute | solution.py:15
  63.0 77.3 %all-to-all-start.1 = ((bf16[24,128,256]{1,2,0:T(8,128)(2,1)}), bf16[24,128,256]{1,2,0:T(8,128)(2,1)S(1)}, u32[]{:S(2)}, u32[]{:S(2)}) async-start(bf16[24,128,256]{1,2,0:T(8,128)(2,1)} %copy.44), calls=%async_computation.1 | async-start | bytes 3145728 | tf_op jit(solution)/shard_map/all_to_all | solution.py:34
  133.9 7.2 %collective-permute-start.1 = (bf16[24,256,128]{2,1,0:T(8,128)(2,1)}, bf16[24,256,128]{2,1,0:T(8,128)(2,1)}, u32[]{:S(2)}, u32[]{:S(2)}) collective-permute-start(bf16[24,256,128]{2,1,0:T(8,128)(2,1)} %bitcast.58), channel_id=1, source_target_pairs={{0,1},{1,0},{2,3},{3,2},{4,5},{5,4},{6,7},{7,6},{8,9},{9,8},{10,11... | collective-permute-start | bytes 4718600 | tf_op jit(solution)/shard_map/ppermute | solution.py:74
  149.8 3.2 %copy-start.1 = (bf16[256,24,2,128]{0,3,2,1:T(8,128)(2,1)S(1)}, bf16[256,24,2,128]{0,3,2,1:T(8,128)(2,1)}, u32[]{:S(2)}) copy-start(bf16[256,24,2,128]{0,3,2,1:T(8,128)(2,1)} %copy.45) | copy-start | bytes 9437188
  153.1 1.0 copy-start.6
  165.7 5.8 %collective-permute-start.2 = (bf16[128,128]{0,1:T(8,128)(2,1)S(1)}, bf16[128,128]{0,1:T(8,128)(2,1)S(1)}, u32[]{:S(2)}, u32[]{:S(2)}) collective-permute-start(bf16[128,128]{0,1:T(8,128)(2,1)S(1)} %slice.75), channel_id=1, source_target_pairs={{48,0},{96,48},{144,96},{192,144},{240,192},{288,240},{336,288},{3... | collective-permute-start | bytes 98312 | tf_op jit(solution)/shard_map/ppermute | solution.py:15
  171.5 47.4 %all-to-all-start.2 = ((bf16[16,392,128]{2,1,0:T(8,128)(2,1)}), bf16[16,392,128]{2,1,0:T(8,128)(2,1)S(1)}, u32[]{:S(2)}, u32[]{:S(2)}) async-start(bf16[16,392,128]{2,1,0:T(8,128)(2,1)} %select_maximum_fusion), calls=%async_computation.2 | async-start | bytes 3211264 | tf_op jit(solution)/shard_map/all_to_all | solution.py:34
  189.2 10.2 %copy-start.3 = (bf16[1,256,128]{1,2,0:T(8,128)(2,1)S(1)}, bf16[1,256,128]{1,2,0:T(8,128)(2,1)}, u32[]{:S(2)}) copy-start(bf16[1,256,128]{1,2,0:T(8,128)(2,1)} %copy-done.2) | copy-start | bytes 196612
  189.2 10.2 %copy-start.5 = (bf16[1,256,128]{1,2,0:T(8,128)(2,1)S(1)}, bf16[1,256,128]{1,2,0:T(8,128)(2,1)}, u32[]{:S(2)}) copy-start(bf16[1,256,128]{1,2,0:T(8,128)(2,1)} %copy-done.4) | copy-start | bytes 196612
  189.2 10.2 %copy-start.7 = (bf16[256,128]{0,1:T(8,128)(2,1)S(1)}, bf16[256,128]{0,1:T(8,128)(2,1)}, u32[]{:S(2)}) copy-start(bf16[256,128]{0,1:T(8,128)(2,1)} %get-tuple-element.35) | copy-start | bytes 196612
Sparse Core Ops, SparseCore 0:
  12.2 121.7 all-gather.2
where the time goes:
time: 228 us; the launch traced here: 227 us
  waiting for transfers between devices  78.1 us (34%)
  local copies, waits for them, and re-layouts  66.6 us (29%)
  starting transfers between devices  33.1 us (15%)
  matrix products  14.3 us (6%)
  between operations  14.3 us (6%)
  other arithmetic  11.1 us (5%)
  blocking collectives  9.95 us (4%)
    all_gather x1, waiting for transfers between devices, local(): same_core = lax.all_gather(grad_out, 'tpo', axis=0)  54.2 us
    all_to_all x2, starting transfers between devices, summed_exchange(): got = lax.all_to_all(sent, axis, 0, 0)  25.4 us
    all_to_all x2, waiting for transfers between devices, summed_exchange(): got = lax.all_to_all(sent, axis, 0, 0)  21.6 us
    reshape x2, local copies, waits for them, and re-layouts, toeplitz_blocks(): tiled[:, :out_rows * (length_all - 1)]  16.5 us
    unnamed x24, local copies, waits for them, and re-layouts  16.3 us
    reshape x2, local copies, waits for them, and re-layouts, local(): halves = partial_out.reshape(chips, cores, block, out_rows)  12.1 us
    all_to_all x1, blocking collectives, local(): pair = lax.all_to_all(halves, 'core', 1, 1)  9.95 us
    reshape x1, local copies, waits for them, and re-layouts, local(): flattened = flipped.reshape(groups, out_rows * (extent + 1))  5.79 us
  transfers between devices with their start and end apart: 6, of which 4 were waited for; matrix products, arithmetic and copies ran while one was open for 28% of the time, Pallas kernels for 0%

commit v1 on v0

--- a/solution.py
+++ b/solution.py
@@ -74,9 +74,10 @@
         partner = lax.ppermute(same_core, "core", [(0, 1), (1, 0)])
         first = lax.axis_index("core") == 0
         both = jnp.stack([jnp.where(first, same_core, partner), jnp.where(first, partner, same_core)], axis=2)
-        full_grad = jnp.transpose(both, (1, 0, 2, 3)).reshape(out_rows, features)
+        full_grad = both
     block_out, full_grad = lax.optimization_barrier((block_out, full_grad))
-    grad_mixed = jnp.einsum("td,cd->tc", full_grad, out_weight, preferred_element_type=jnp.float32)
+    weight_blocks = out_weight.reshape(channels, chips, cores, block)
+    grad_mixed = jnp.einsum("jtkl,cjkl->tc", full_grad, weight_blocks, preferred_element_type=jnp.float32)
     grad_filtered = (grad_mixed * query_rows).astype(jnp.bfloat16)
     grad_query = (grad_mixed * filtered).astype(jnp.bfloat16)
     following = shifted(grad_filtered[:taps_count], "ctx", -1)
@@ -100,7 +101,7 @@
     filter_term = jnp.sum(diagonals, axis=1) / math.sqrt(sequence * group_size)
     weight_scale = 1.0 / math.sqrt(sequence)
     weight_term = (
-        jnp.einsum("tc,td->dc", mixed_rows, full_grad, preferred_element_type=jnp.float32)
+        jnp.einsum("tc,jtkl->jklc", mixed_rows, full_grad, preferred_element_type=jnp.float32)
         * weight_scale
     )
     own_cols = features // ctx_count

time: 228 us -> 226 us (level)
  the two profiles are of different devices: /device:TPU:10 before, /device:TPU:8 now
where the time goes in v1:
time: 226 us; the launch traced here: 225 us
  waiting for transfers between devices  85.8 us (38%)
  local copies, waits for them, and re-layouts  57.4 us (25%)
  starting transfers between devices  34.8 us (15%)
  between operations  14.3 us (6%)
  other arithmetic  12.3 us (5%)
  matrix products  10.7 us (5%)
  blocking collectives  9.96 us (4%)
    all_gather x1, waiting for transfers between devices, local(): same_core = lax.all_gather(grad_out, 'tpo', axis=0)  60.3 us
    all_to_all x2, starting transfers between devices, summed_exchange(): got = lax.all_to_all(sent, axis, 0, 0)  25.8 us
    all_to_all x2, waiting for transfers between devices, summed_exchange(): got = lax.all_to_all(sent, axis, 0, 0)  25.4 us
    reshape x2, local copies, waits for them, and re-layouts, toeplitz_blocks(): tiled[:, :out_rows * (length_all - 1)]  14.4 us
    unnamed x22, local copies, waits for them, and re-layouts  13.6 us
    reshape x2, local copies, waits for them, and re-layouts, local(): halves = partial_out.reshape(chips, cores, block, out_rows)  12.2 us
    all_to_all x1, blocking collectives, local(): pair = lax.all_to_all(halves, 'core', 1, 1)  9.96 us
    ppermute x2, starting transfers between devices, shifted(): lax.ppermute(value, axis, [(source, source + steps) for source in range(f...  7.04 us
  transfers between devices with their start and end apart: 6, of which 2 were waited for; matrix products, arithmetic and copies ran while one was open for 27% of the time, Pallas kernels for 0%

profile of v1, /device:TPU:8, one launch (start us, length us, event | category | flops | bytes accessed | tf_op | source)
XLA Modules:
  0.0 225.2 jit_solution(14257172049569437518)
XLA Ops:
  7.2 0.9 fusion.24
  8.4 3.5 %collective-permute-start = (bf16[128,128]{0,1:T(8,128)(2,1)S(1)}, bf16[128,128]{0,1:T(8,128)(2,1)S(1)}, u32[]{:S(2)}, u32[]{:S(2)}) collective-permute-start(bf16[128,128]{0,1:T(8,128)(2,1)S(1)} %slice_bitcast_fusion.1), channel_id=1, source_target_pairs={{0,48},{48,96},{96,144},{144,192},{192,240},{240,288},{288,336},{3... | collective-permute-start | bytes 98312 | tf_op jit(solution)/shard_map/ppermute | solution.py:15
  13.3 5.4 %reshape.81 = bf16[1308672]{0:T(1024)(128)(2,1)} reshape(bf16[8,163584]{1,0:T(8,128)(2,1)S(1)} %slice.73) | data formatting | bytes 5234688
  18.7 7.2 %reshape.66 = bf16[8,256,639]{2,1,0:T(8,128)(2,1)S(1)} reshape(bf16[1308672]{0:T(1024)(128)(2,1)} %reshape.81) | data formatting | bytes 5234688 | tf_op jit(solution)/shard_map/reshape | solution.py:28
  26.6 0.8 copy-done
  27.4 3.7 %convolution_bitcast_fusion = f32[6144,256]{0,1:T(8,128)} fusion(bf16[256,128]{0,1:T(8,128)(2,1)S(1)} %fusion.12, bf16[128,6144]{1,0:T(8,128)(2,1)S(1)} %copy-done), kind=kOutput, calls=%fused_computation | convolution fusion | flops 402653184 | bytes 7929856 | tf_op jit(solution)/shard_map/cd,tc->dt/dot_general | solution.py:61
  31.1 9.0 %reshape.68 = f32[24,2,128,256]{2,1,0,3:T(2,128)} reshape(f32[6144,256]{0,1:T(8,128)} %convolution_bitcast_fusion) | data formatting | bytes 12582912 | tf_op jit(solution)/shard_map/reshape | solution.py:63
  40.0 3.2 %copy.53 = f32[24,2,128,256]{2,0,3,1:T(8,128)S(1)} copy(f32[24,2,128,256]{2,1,0,3:T(2,128)} %reshape.68) | data formatting | bytes 12582912 | tf_op jit(solution)/shard_map/reshape | solution.py:63
  43.2 10.0 %all_to_all.15 = f32[24,2,128,256]{2,0,3,1:T(8,128)} all-to-all(f32[24,2,128,256]{2,0,3,1:T(8,128)S(1)} %copy.53), channel_id=1, replica_groups=mesh['ctx'=16,'tpo'=24,'core'=2] {'core'}, dimensions={1} | all-to-all | bytes 12582912 | tf_op jit(solution)/shard_map/all_to_all | solution.py:64
  53.2 3.5 %reduce_sum.39 = bf16[24,128,256]{1,0,2:T(8,128)(2,1)S(1)} reduce(f32[24,2,128,256]{2,0,3,1:T(8,128)} %all_to_all.15, f32[]{:T(128)} %constant.5.clone.1), dimensions={1}, to_apply=%region_0.1 | reduce | flops 786432 | bytes 7864324 | tf_op jit(solution)/shard_map/reduce_sum | solution.py:65
  56.7 1.5 copy.55
  58.2 16.3 %all-to-all-start.1 = ((bf16[24,128,256]{1,2,0:T(8,128)(2,1)}), bf16[24,128,256]{1,2,0:T(8,128)(2,1)S(1)}, u32[]{:S(2)}, u32[]{:S(2)}) async-start(bf16[24,128,256]{1,2,0:T(8,128)(2,1)} %copy.55), calls=%async_computation.1 | async-start | bytes 3145728 | tf_op jit(solution)/shard_map/all_to_all | solution.py:34
  74.5 60.3 %all-gather.3.cloned.1.call-done = bf16[6144,128]{1,0:T(8,128)(2,1)} async-done(((bf16[256,128]{1,0:T(8,128)(2,1)}), bf16[6144,128]{1,0:T(8,128)(2,1)}) %all-gather.3.cloned.1.call-update) | async-done | bytes 1572880 | tf_op jit(solution)/shard_map/all_gather | solution.py:73
  134.8 2.6 %copy.57 = bf16[24,256,128]{1,2,0:T(8,128)(2,1)} copy(bf16[24,256,128]{2,1,0:T(8,128)(2,1)} %bitcast.60) | data formatting | bytes 3145728 | tf_op jit(solution)/shard_map/all_gather | solution.py:73
  137.4 1.9 collective-permute-start.1
  139.3 4.1 %reshape.69 = bf16[128,24,2,128]{3,2,1,0:T(2,128)(2,1)S(1)} reshape(bf16[128,6144]{1,0:T(8,128)(2,1)} %param.6) | data formatting | bytes 3145728 | tf_op jit(solution)/shard_map/reshape | solution.py:79
  143.4 1.4 rev.7
  144.8 0.8 reduce_sum.40
  145.7 2.1 select_bitcast_fusion.1
  148.1 2.2 convolution_multiply_fusion
  150.2 1.2 fusion.14
  151.4 2.6 %fusion.15 = f32[8,256,385]{2,1,0:T(8,128)} fusion(bf16[256,8,16]{0,2,1:T(8,128)(2,1)S(1)} %bitcast.63, bf16[384,8,16]{0,2,1:T(8,128)(2,1)S(1)} %copy-done.5), kind=kOutput, calls=%fused_computation.30 | convolution fusion | flops 25231360 | bytes 3317760 | tf_op jit(solution)/shard_map/tgc,sgc->gts/dot_general | solution.py:90
  154.1 4.1 %reshape.75 = f32[8,98560]{1,0:T(8,128)S(1)} reshape(f32[8,256,385]{2,1,0:T(8,128)} %fusion.15) | data formatting | bytes 6307840 | tf_op jit(solution)/shard_map/reshape | solution.py:96
  158.2 0.9 slice.78
  159.5 3.6 %collective-permute-start.2 = (bf16[128,128]{0,1:T(8,128)(2,1)S(1)}, bf16[128,128]{0,1:T(8,128)(2,1)S(1)}, u32[]{:S(2)}, u32[]{:S(2)}) collective-permute-start(bf16[128,128]{0,1:T(8,128)(2,1)S(1)} %slice.75), channel_id=1, source_target_pairs={{48,0},{96,48},{144,96},{192,144},{240,192},{288,240},{336,288},{3... | collective-permute-start | bytes 98312 | tf_op jit(solution)/shard_map/ppermute | solution.py:15
  163.0 2.7 %select_maximum_fusion = bf16[16,392,128]{2,1,0:T(8,128)(2,1)} fusion(bf16[16,8,8]{2,1,0:T(8,128)(2,1)S(1)} %copy.76, bf16[16,384,128]{2,1,0:T(8,128)(2,1)} %bitcast.58), kind=kLoop, calls=%fused_computation.1 | loop fusion | flops 4816896 | bytes 3180544 | tf_op jit(solution)/shard_map/concatenate | solution.py:112
  165.8 9.5 %all-to-all-start.2 = ((bf16[16,392,128]{2,1,0:T(8,128)(2,1)}), bf16[16,392,128]{2,1,0:T(8,128)(2,1)}, u32[]{:S(2)}, u32[]{:S(2)}) async-start(bf16[16,392,128]{2,1,0:T(8,128)(2,1)} %select_maximum_fusion), calls=%async_computation.2 | async-start | bytes 3211264 | tf_op jit(solution)/shard_map/all_to_all | solution.py:34
  175.7 5.4 %reshape.83 = bf16[1308672]{0:T(1024)(128)(2,1)} reshape(bf16[8,163584]{1,0:T(8,128)(2,1)S(1)} %slice.76) | data formatting | bytes 5234688
  181.2 7.2 %reshape.71 = bf16[8,256,639]{2,1,0:T(8,128)(2,1)S(1)} reshape(bf16[1308672]{0:T(1024)(128)(2,1)} %reshape.83) | data formatting | bytes 5234688 | tf_op jit(solution)/shard_map/reshape | solution.py:28
  189.0 0.8 copy.65
  189.8 25.4 %all-to-all-done.2 = bf16[16,392,128]{2,1,0:T(8,128)(2,1)} async-done(((bf16[16,392,128]{2,1,0:T(8,128)(2,1)}), bf16[16,392,128]{2,1,0:T(8,128)(2,1)}, u32[]{:S(2)}, u32[]{:S(2)}) %all-to-all-start.2) | async-done | bytes 1605664 | tf_op jit(solution)/shard_map/all_to_all | solution.py:34
  215.3 1.7 convert_reduce_fusion
  (49 shorter events, 5.4 us)
Async XLA Ops:
  7.2 127.7 %all-gather.3.cloned.1.call-start = ((), (), s32[]{:S(2)}) async-start(), calls=%async_computation.3 | async-start | bytes 1638400 | tf_op jit(solution)/shard_map/all_gather | solution.py:73
  8.2 4.8 %copy-start.1 = (bf16[1,256,128]{1,2,0:T(8,128)(2,1)}, bf16[1,256,128]{1,2,0:T(8,128)(2,1)S(1)}, u32[]{:S(2)}) copy-start(bf16[1,256,128]{1,2,0:T(8,128)(2,1)S(1)} %copy.74) | copy-start | bytes 196612
  8.4 4.7 %copy-start.3 = (bf16[1,256,128]{1,2,0:T(8,128)(2,1)}, bf16[1,256,128]{1,2,0:T(8,128)(2,1)S(1)}, u32[]{:S(2)}) copy-start(bf16[1,256,128]{1,2,0:T(8,128)(2,1)S(1)} %copy.75) | copy-start | bytes 196612
  8.4 17.6 %collective-permute-start = (bf16[128,128]{0,1:T(8,128)(2,1)S(1)}, bf16[128,128]{0,1:T(8,128)(2,1)S(1)}, u32[]{:S(2)}, u32[]{:S(2)}) collective-permute-start(bf16[128,128]{0,1:T(8,128)(2,1)S(1)} %slice_bitcast_fusion.1), channel_id=1, source_target_pairs={{0,48},{48,96},{96,144},{144,192},{192,240},{240,288},{288,336},{3... | collective-permute-start | bytes 98312 | tf_op jit(solution)/shard_map/ppermute | solution.py:15
  26.0 1.4 copy-start
  58.2 86.6 %all-to-all-start.1 = ((bf16[24,128,256]{1,2,0:T(8,128)(2,1)}), bf16[24,128,256]{1,2,0:T(8,128)(2,1)S(1)}, u32[]{:S(2)}, u32[]{:S(2)}) async-start(bf16[24,128,256]{1,2,0:T(8,128)(2,1)} %copy.55), calls=%async_computation.1 | async-start | bytes 3145728 | tf_op jit(solution)/shard_map/all_to_all | solution.py:34
  137.4 8.3 %collective-permute-start.1 = (bf16[24,256,128]{1,2,0:T(8,128)(2,1)}, bf16[24,256,128]{1,2,0:T(8,128)(2,1)}, u32[]{:S(2)}, u32[]{:S(2)}) collective-permute-start(bf16[24,256,128]{1,2,0:T(8,128)(2,1)} %copy.57), channel_id=1, source_target_pairs={{0,1},{1,0},{2,3},{3,2},{4,5},{5,4},{6,7},{7,6},{8,9},{9,8},{10,11... | collective-permute-start | bytes 4718600 | tf_op jit(solution)/shard_map/ppermute | solution.py:74
  150.2 1.2 copy-start.5
  159.5 6.3 %collective-permute-start.2 = (bf16[128,128]{0,1:T(8,128)(2,1)S(1)}, bf16[128,128]{0,1:T(8,128)(2,1)S(1)}, u32[]{:S(2)}, u32[]{:S(2)}) collective-permute-start(bf16[128,128]{0,1:T(8,128)(2,1)S(1)} %slice.75), channel_id=1, source_target_pairs={{48,0},{96,48},{144,96},{192,144},{240,192},{288,240},{336,288},{3... | collective-permute-start | bytes 98312 | tf_op jit(solution)/shard_map/ppermute | solution.py:15
  165.8 49.5 %all-to-all-start.2 = ((bf16[16,392,128]{2,1,0:T(8,128)(2,1)}), bf16[16,392,128]{2,1,0:T(8,128)(2,1)}, u32[]{:S(2)}, u32[]{:S(2)}) async-start(bf16[16,392,128]{2,1,0:T(8,128)(2,1)} %select_maximum_fusion), calls=%async_computation.2 | async-start | bytes 3211264 | tf_op jit(solution)/shard_map/all_to_all | solution.py:34
  181.1 7.8 %copy-start.2 = (bf16[1,256,128]{1,2,0:T(8,128)(2,1)S(1)}, bf16[1,256,128]{1,2,0:T(8,128)(2,1)}, u32[]{:S(2)}) copy-start(bf16[1,256,128]{1,2,0:T(8,128)(2,1)} %copy-done.1) | copy-start | bytes 196612
  181.1 7.8 %copy-start.4 = (bf16[1,256,128]{1,2,0:T(8,128)(2,1)S(1)}, bf16[1,256,128]{1,2,0:T(8,128)(2,1)}, u32[]{:S(2)}) copy-start(bf16[1,256,128]{1,2,0:T(8,128)(2,1)} %copy-done.3) | copy-start | bytes 196612
  181.2 7.8 %copy-start.6 = (bf16[256,128]{0,1:T(8,128)(2,1)S(1)}, bf16[256,128]{0,1:T(8,128)(2,1)}, u32[]{:S(2)}) copy-start(bf16[256,128]{0,1:T(8,128)(2,1)} %get-tuple-element.31) | copy-start | bytes 196612
Sparse Core Ops, SparseCore 0:
  12.1 122.7 all-gather.2

commit v2 on v1

--- a/solution.py
+++ b/solution.py
@@ -58,11 +58,11 @@
         "gts,sgc->tgc", blocks, extended, preferred_element_type=jnp.float32
     ).reshape(out_rows, channels)
     mixed_rows = (query_rows * filtered).astype(jnp.bfloat16)
-    partial_out = jnp.einsum("cd,tc->dt", out_weight, mixed_rows, preferred_element_type=jnp.float32)
     block = features // tp_count
-    halves = partial_out.reshape(chips, cores, block, out_rows)
-    pair = lax.all_to_all(halves, "core", 1, 1)
-    chip_sum = jnp.sum(pair, axis=1)
+    weight_blocks = out_weight.reshape(channels, chips, cores, block)
+    halves = jnp.einsum("cjkl,tc->kjlt", weight_blocks, mixed_rows, preferred_element_type=jnp.float32)
+    pair = lax.all_to_all(halves, "core", 0, 0)
+    chip_sum = jnp.sum(pair, axis=0)
     own_features = summed_exchange(chip_sum, "tpo")
     block_out = own_features.T.astype(jnp.bfloat16)
     if GATHER_BY_A2A:
@@ -76,7 +76,6 @@
         both = jnp.stack([jnp.where(first, same_core, partner), jnp.where(first, partner, same_core)], axis=2)
         full_grad = both
     block_out, full_grad = lax.optimization_barrier((block_out, full_grad))
-    weight_blocks = out_weight.reshape(channels, chips, cores, block)
     grad_mixed = jnp.einsum("jtkl,cjkl->tc", full_grad, weight_blocks, preferred_element_type=jnp.float32)
     grad_filtered = (grad_mixed * query_rows).astype(jnp.bfloat16)
     grad_query = (grad_mixed * filtered).astype(jnp.bfloat16)

time: 226 us -> 228 us (level)
  local copies, waits for them, and re-layouts: 57.4 us -> 41.9 us
  waiting for transfers between devices: 85.8 us -> 101 us
    all_gather x1, waiting for transfers between devices: 60.3 us -> 72.9 us  [local(): same_core = lax.all_gather(grad_out, 'tpo', axis=0)]
    reshape x2 -> x0, local copies, waits for them, and re-layouts: 12.2 us -> none  [local(): halves = partial_out.reshape(chips, cores, block, out_rows)]
    reshape x1, local copies, waits for them, and re-layouts: 4.07 us -> 1.14 us  [local(): weight_blocks = out_weight.reshape(channels, chips, cores, block)]
    dot_general x1, matrix products: 3.66 us -> 1 us  [local(): jnp.einsum('cjkl,tc->kjlt', weight_blocks, mixed_rows, preferred_element_...]
    all_to_all x2, starting transfers between devices: 25.8 us -> 28.2 us  [summed_exchange(): got = lax.all_to_all(sent, axis, 0, 0)]
    ppermute x1, waiting for transfers between devices: 0.01 us -> 2.33 us  [local(): partner = lax.ppermute(same_core, 'core', [(0, 1), (1, 0)])]
    unnamed x22 -> x16, local copies, waits for them, and re-layouts: 13.6 us -> 13.4 us
  transfers between devices with their start and end apart: 6 -> 6, of which waited for: 2 -> 4; matrix products, arithmetic and copies ran while one was open for 27% -> 20% of each run, Pallas kernels for 0% -> 0%
where the time goes in v2:
time: 228 us
  waiting for transfers between devices  101 us (44%)
  local copies, waits for them, and re-layouts  41.9 us (18%)
  starting transfers between devices  36.4 us (16%)
  between operations  14.3 us (6%)
  other arithmetic  13.7 us (6%)
  matrix products  10.1 us (4%)
  blocking collectives  9.97 us (4%)
    all_gather x1, waiting for transfers between devices, local(): same_core = lax.all_gather(grad_out, 'tpo', axis=0)  72.9 us
    all_to_all x2, starting transfers between devices, summed_exchange(): got = lax.all_to_all(sent, axis, 0, 0)  28.2 us
    all_to_all x2, waiting for transfers between devices, summed_exchange(): got = lax.all_to_all(sent, axis, 0, 0)  25.4 us
    reshape x2, local copies, waits for them, and re-layouts, toeplitz_blocks(): tiled[:, :out_rows * (length_all - 1)]  15.6 us
    unnamed x16, local copies, waits for them, and re-layouts  13.4 us
    all_to_all x1, blocking collectives, local(): pair = lax.all_to_all(halves, 'core', 0, 0)  9.97 us
    ppermute x2, starting transfers between devices, shifted(): lax.ppermute(value, axis, [(source, source + steps) for source in range(f...  6.08 us
    reduce_sum x1, other arithmetic, local(): chip_sum = jnp.sum(pair, axis=0)  4.92 us
  transfers between devices with their start and end apart: 6, of which 4 were waited for; matrix products, arithmetic and copies ran while one was open for 20% of the time, Pallas kernels for 0%

profile of v2, /device:TPU:8, one launch (start us, length us, event | category | flops | bytes accessed | tf_op | source)
XLA Modules:
  0.0 227.6 jit_solution(4723253715809578911)
XLA Ops:
  7.2 0.9 fusion.26
  8.4 3.5 %collective-permute-start = (bf16[128,128]{0,1:T(8,128)(2,1)S(1)}, bf16[128,128]{0,1:T(8,128)(2,1)S(1)}, u32[]{:S(2)}, u32[]{:S(2)}) collective-permute-start(bf16[128,128]{0,1:T(8,128)(2,1)S(1)} %slice_bitcast_fusion.1), channel_id=1, source_target_pairs={{0,48},{48,96},{96,144},{144,192},{192,240},{240,288},{288,336},{3... | collective-permute-start | bytes 98312 | tf_op jit(solution)/shard_map/ppermute | solution.py:15
  11.9 0.7 convert_element_type.77
  13.3 5.4 %reshape.83 = bf16[1308672]{0:T(1024)(128)(2,1)} reshape(bf16[8,163584]{1,0:T(8,128)(2,1)S(1)} %slice.73) | data formatting | bytes 5234688
  18.7 8.3 %reshape.67 = bf16[8,256,639]{2,1,0:T(8,128)(2,1)} reshape(bf16[1308672]{0:T(1024)(128)(2,1)} %reshape.83) | data formatting | bytes 5234688 | tf_op jit(solution)/shard_map/reshape | solution.py:28
  27.1 1.1 reshape.68
  28.3 2.6 %fusion.16 = (bf16[256,8,16]{0,2,1:T(8,128)(2,1)S(1)}, f32[8,16,256]{2,1,0:T(8,128)}) fusion(bf16[384,8,16]{0,2,1:T(8,128)(2,1)S(1)} %bitcast.69, bf16[8,256,639]{2,1,0:T(8,128)(2,1)} %reshape.67, bf16[256,8,16]{0,2,1:T(8,128)(2,1)S(1)} %bitcast.72), kind=kOutput, calls=%fused_computation.32 | convolution fusion | flops 25264128 | bytes 1933312 | tf_op jit(solution)/shard_map/gts,sgc->tgc/dot_general | solution.py:57
  30.9 1.0 convolution_bitcast_fusion
  31.9 0.7 copy.43
  32.6 10.0 %all_to_all.15 = f32[2,24,128,256]{2,3,1,0:T(8,128)} all-to-all(f32[2,24,128,256]{2,3,1,0:T(8,128)S(1)} %copy.43), channel_id=1, replica_groups=mesh['ctx'=16,'tpo'=24,'core'=2] {'core'}, dimensions={0} | all-to-all | bytes 12582912 | tf_op jit(solution)/shard_map/all_to_all | solution.py:64
  42.5 4.9 %reduce_sum.39 = bf16[24,128,256]{1,2,0:T(8,128)(2,1)} reduce(f32[2,24,128,256]{2,3,1,0:T(8,128)} %all_to_all.15, f32[]{:T(128)} %constant.5.clone.1), dimensions={0}, to_apply=%region_0.1 | reduce | flops 786432 | bytes 7864324 | tf_op jit(solution)/shard_map/reduce_sum | solution.py:65
  47.5 16.3 %all-to-all-start.1 = ((bf16[24,128,256]{1,2,0:T(8,128)(2,1)}), bf16[24,128,256]{1,2,0:T(8,128)(2,1)S(1)}, u32[]{:S(2)}, u32[]{:S(2)}) async-start(bf16[24,128,256]{1,2,0:T(8,128)(2,1)} %reduce_sum.39), calls=%async_computation.1 | async-start | bytes 3145728 | tf_op jit(solution)/shard_map/all_to_all | solution.py:34
  63.8 72.9 %all-gather.3.cloned.1.call-done = bf16[6144,128]{1,0:T(8,128)(2,1)} async-done(((bf16[256,128]{1,0:T(8,128)(2,1)}), bf16[6144,128]{1,0:T(8,128)(2,1)}) %all-gather.3.cloned.1.call-update) | async-done | bytes 1572880 | tf_op jit(solution)/shard_map/all_gather | solution.py:73
  136.7 2.6 %copy.46 = bf16[24,256,128]{1,2,0:T(8,128)(2,1)} copy(bf16[24,256,128]{2,1,0:T(8,128)(2,1)} %bitcast.68) | data formatting | bytes 3145728 | tf_op jit(solution)/shard_map/all_gather | solution.py:73
  139.3 2.1 collective-permute-start.1
  141.8 0.8 reduce_sum.40
  142.6 2.3 %collective-permute-done.1 = bf16[24,256,128]{1,2,0:T(8,128)(2,1)} collective-permute-done((bf16[24,256,128]{1,2,0:T(8,128)(2,1)}, bf16[24,256,128]{1,2,0:T(8,128)(2,1)}, u32[]{:S(2)}, u32[]{:S(2)}) %collective-permute-start.1) | collective-permute-done | bytes 1572896 | tf_op jit(solution)/shard_map/ppermute | solution.py:74
  145.0 2.1 select_bitcast_fusion.1
  148.0 1.2 fusion.14
  149.2 2.2 convolution_multiply_fusion
  151.9 2.6 %fusion.17 = f32[8,256,385]{2,1,0:T(8,128)} fusion(bf16[256,8,16]{0,2,1:T(8,128)(2,1)S(1)} %bitcast.71, bf16[384,8,16]{0,2,1:T(8,128)(2,1)S(1)} %rev.7), kind=kOutput, calls=%fused_computation.33 | convolution fusion | flops 25231360 | bytes 3317760 | tf_op jit(solution)/shard_map/tgc,sgc->gts/dot_general | solution.py:89
  154.6 4.1 %reshape.75 = f32[8,98560]{1,0:T(8,128)S(1)} reshape(f32[8,256,385]{2,1,0:T(8,128)} %fusion.17) | data formatting | bytes 6307840 | tf_op jit(solution)/shard_map/reshape | solution.py:95
  158.7 0.9 slice.78
  160.0 2.6 %collective-permute-start.2 = (bf16[128,128]{0,1:T(8,128)(2,1)S(1)}, bf16[128,128]{0,1:T(8,128)(2,1)S(1)}, u32[]{:S(2)}, u32[]{:S(2)}) collective-permute-start(bf16[128,128]{0,1:T(8,128)(2,1)S(1)} %copy-done.3), channel_id=1, source_target_pairs={{48,0},{96,48},{144,96},{192,144},{240,192},{288,240},{336,288},{3... | collective-permute-start | bytes 98312 | tf_op jit(solution)/shard_map/ppermute | solution.py:15
  162.6 2.7 %select_maximum_fusion = bf16[16,392,128]{2,1,0:T(8,128)(2,1)} fusion(bf16[16,8,8]{2,1,0:T(8,128)(2,1)S(1)} %copy.67, bf16[16,384,128]{2,1,0:T(8,128)(2,1)} %bitcast.66), kind=kLoop, calls=%fused_computation | loop fusion | flops 4816896 | bytes 3180544 | tf_op jit(solution)/shard_map/concatenate | solution.py:111
  165.8 11.9 %all-to-all-start.2 = ((bf16[16,392,128]{2,1,0:T(8,128)(2,1)}), bf16[16,392,128]{2,1,0:T(8,128)(2,1)}, u32[]{:S(2)}, u32[]{:S(2)}) async-start(bf16[16,392,128]{2,1,0:T(8,128)(2,1)} %select_maximum_fusion), calls=%async_computation.2 | async-start | bytes 3211264 | tf_op jit(solution)/shard_map/all_to_all | solution.py:34
  178.2 5.4 %reshape.85 = bf16[1308672]{0:T(1024)(128)(2,1)} reshape(bf16[8,163584]{1,0:T(8,128)(2,1)S(1)} %slice.76) | data formatting | bytes 5234688
  183.6 7.2 %reshape.71 = bf16[8,256,639]{2,1,0:T(8,128)(2,1)S(1)} reshape(bf16[1308672]{0:T(1024)(128)(2,1)} %reshape.85) | data formatting | bytes 5234688 | tf_op jit(solution)/shard_map/reshape | solution.py:28
  191.4 0.8 copy.54
  192.2 25.4 %all-to-all-done.2 = bf16[16,392,128]{2,1,0:T(8,128)(2,1)} async-done(((bf16[16,392,128]{2,1,0:T(8,128)(2,1)}), bf16[16,392,128]{2,1,0:T(8,128)(2,1)}, u32[]{:S(2)}, u32[]{:S(2)}) %all-to-all-start.2) | async-done | bytes 1605664 | tf_op jit(solution)/shard_map/all_to_all | solution.py:34
  217.6 1.7 convert_reduce_fusion
  219.9 0.8 copy.55
  (40 shorter events, 5.4 us)
Async XLA Ops:
  7.2 129.6 %all-gather.3.cloned.1.call-start = ((), (), s32[]{:S(2)}) async-start(), calls=%async_computation.3 | async-start | bytes 1638400 | tf_op jit(solution)/shard_map/all_gather | solution.py:73
  8.4 19.8 %collective-permute-start = (bf16[128,128]{0,1:T(8,128)(2,1)S(1)}, bf16[128,128]{0,1:T(8,128)(2,1)S(1)}, u32[]{:S(2)}, u32[]{:S(2)}) collective-permute-start(bf16[128,128]{0,1:T(8,128)(2,1)S(1)} %slice_bitcast_fusion.1), channel_id=1, source_target_pairs={{0,48},{48,96},{96,144},{144,192},{192,240},{240,288},{288,336},{3... | collective-permute-start | bytes 98312 | tf_op jit(solution)/shard_map/ppermute | solution.py:15
  18.7 8.3 %copy-start = (bf16[128,6144]{1,0:T(8,128)(2,1)S(1)}, bf16[128,6144]{1,0:T(8,128)(2,1)}, u32[]{:S(2)}) copy-start(bf16[128,6144]{1,0:T(8,128)(2,1)} %param.6) | copy-start | bytes 4718596
  47.5 94.3 %all-to-all-start.1 = ((bf16[24,128,256]{1,2,0:T(8,128)(2,1)}), bf16[24,128,256]{1,2,0:T(8,128)(2,1)S(1)}, u32[]{:S(2)}, u32[]{:S(2)}) async-start(bf16[24,128,256]{1,2,0:T(8,128)(2,1)} %reduce_sum.39), calls=%async_computation.1 | async-start | bytes 3145728 | tf_op jit(solution)/shard_map/all_to_all | solution.py:34
  139.3 5.6 %collective-permute-start.1 = (bf16[24,256,128]{1,2,0:T(8,128)(2,1)}, bf16[24,256,128]{1,2,0:T(8,128)(2,1)}, u32[]{:S(2)}, u32[]{:S(2)}) collective-permute-start(bf16[24,256,128]{1,2,0:T(8,128)(2,1)} %copy.46), channel_id=1, source_target_pairs={{0,1},{1,0},{2,3},{3,2},{4,5},{5,4},{6,7},{7,6},{8,9},{9,8},{10,11... | collective-permute-start | bytes 4718600 | tf_op jit(solution)/shard_map/ppermute | solution.py:74
  147.0 0.9 copy-start.1
  158.7 1.3 copy-start.3
  160.0 5.8 %collective-permute-start.2 = (bf16[128,128]{0,1:T(8,128)(2,1)S(1)}, bf16[128,128]{0,1:T(8,128)(2,1)S(1)}, u32[]{:S(2)}, u32[]{:S(2)}) collective-permute-start(bf16[128,128]{0,1:T(8,128)(2,1)S(1)} %copy-done.3), channel_id=1, source_target_pairs={{48,0},{96,48},{144,96},{192,144},{240,192},{288,240},{336,288},{3... | collective-permute-start | bytes 98312 | tf_op jit(solution)/shard_map/ppermute | solution.py:15
  165.8 51.8 %all-to-all-start.2 = ((bf16[16,392,128]{2,1,0:T(8,128)(2,1)}), bf16[16,392,128]{2,1,0:T(8,128)(2,1)}, u32[]{:S(2)}, u32[]{:S(2)}) async-start(bf16[16,392,128]{2,1,0:T(8,128)(2,1)} %select_maximum_fusion), calls=%async_computation.2 | async-start | bytes 3211264 | tf_op jit(solution)/shard_map/all_to_all | solution.py:34
  183.6 7.8 %copy-start.2 = (bf16[256,128]{0,1:T(8,128)(2,1)S(1)}, bf16[256,128]{0,1:T(8,128)(2,1)}, u32[]{:S(2)}) copy-start(bf16[256,128]{0,1:T(8,128)(2,1)} %get-tuple-element.28) | copy-start | bytes 196612
Sparse Core Ops, SparseCore 0:
  12.0 124.6 all-gather.2
